TPU v7x, 256 devices: a whole 4x4x8 slice. The times are simulated.
256 devices in a mesh: req: 32 (over x, y, core), tp: 8 (over z).
Axes of the slice: x: 4, y: 4, z: 8, core: 2. Of those that a mesh axis runs over, the one named last changes fastest.
Arguments:
- query: bfloat16 [768, 4096], P('req', 'tp'), may hold values from -102 to 102
- new_key: bfloat16 [768, 1024], P('req', 'tp'), may hold values from -6 to 6
- new_value: bfloat16 [768, 1024], P('req', 'tp'), may hold values from -6 to 6
- prefix_key: bfloat16 [64, 6144, 1024], P('req', None, 'tp'), may hold values from -6 to 6
- prefix_value: bfloat16 [64, 6144, 1024], P('req', None, 'tp'), may hold values from -6 to 6
- suffix_key: bfloat16 [768, 128, 1024], P('req', None, 'tp'), may hold values from -6 to 6
- suffix_value: bfloat16 [768, 128, 1024], P('req', None, 'tp'), may hold values from -6 to 6
- group_ids: int32 [768], replicated, may hold values from 0 to 63, as said below
- prompt_len: int32 [64], P('req'), may hold values from 768 to 6144, as said below
- suffix_len: int32 [768], replicated, may hold values from 1 to 128, as said below
- o_weight: bfloat16 [4096, 4096], P('tp'), may hold values from -0.09375 to 0.09375
- residual: bfloat16 [768, 4096], P('req'), may hold values from -0.29882812 to 0.29882812
- norm_gain: bfloat16 [4096], replicated, may hold values from 0.5 to 1.5
Outputs:
- hidden: bfloat16 [768, 4096], P('req')
- normed: bfloat16 [768, 4096], P('req')
Inputs may be any that keep to these rules, and one draw needn't show every extreme that they name: Request r belongs to group group_ids[r]; groups 2k to 2k + 1 at a time are held together (group // 2 names the holder). Among each aligned block of 24 requests, every holder that appears is named by exactly 2 of them. `prompt_len`: some group has exactly 6144. `suffix_len`: some request has exactly 128.
All inputs are finite; a program needn't handle non-finite values.
Results may differ from a plain program's by a relative error of at most 0.008.
Values may be sent and summed in bfloat16 or wider, within the bound.
No kernel may reach another device: no remote copies, remote signals or barrier semaphores. Data moves between devices by JAX's collectives and lax.ppermute only.
A program may use at most 64 MiB of HBM per device.

v0:
```python
import math
import jax
import jax.numpy as jnp
from jax import lax
from jax.sharding import PartitionSpec as P

HD = 128
WIN = 4096
SINKS = 4
FAR_BELOW = -1e30
NORM_EPS = 1e-06


def prefix_attend(
    rows_query, row_group, row_suffix, prefix_key, prefix_value, prompt_len, first_group, blocks
):
    row_count = rows_query.shape[0]
    groups_dev = prefix_key.shape[0]
    prompt_max = prefix_key.shape[1]
    kv_dev = prefix_key.shape[2] // HD
    heads_dev = rows_query.shape[1] // HD
    repeat = heads_dev // kv_dev
    block_len = min(512, prompt_max)
    score_scale = 1.0 / math.sqrt(HD)
    local_group = row_group - first_group
    owned = (local_group >= 0) & (local_group < groups_dev)
    member = local_group[:, None] == jnp.arange(groups_dev, dtype=jnp.int32)[None, :]
    row_prompt = jnp.sum(jnp.where(member, prompt_len[None, :], 0), axis=1)
    row_low = row_prompt + row_suffix - WIN + 1
    queries = rows_query.reshape(row_count, kv_dev, repeat, HD)

    def key_step(block_index, loop_state):
        running, weight_sum, weighted = loop_state
        key_start = block_index * block_len
        key_block = lax.dynamic_slice_in_dim(prefix_key, key_start, block_len, 1).reshape(
            groups_dev, block_len, kv_dev, HD
        )
        value_block = lax.dynamic_slice_in_dim(prefix_value, key_start, block_len, 1).reshape(
            groups_dev, block_len, kv_dev, HD
        )
        scores = (
            jnp.einsum("rkhd,gpkd->rkhgp", queries, key_block, preferred_element_type=jnp.float32)
            * score_scale
        )
        positions = key_start + jnp.arange(block_len, dtype=jnp.int32)
        inside = positions[None, :] < prompt_len[:, None]
        window = (positions[None, :] < SINKS) | (positions[None, :] >= row_low[:, None])
        usable = member[:, :, None] & inside[None, :, :] & window[:, None, :]
        usable = usable[:, None, None, :, :]
        masked = jnp.where(usable, scores, FAR_BELOW)
        updated = jnp.maximum(running, jnp.max(masked, axis=(3, 4)))
        weights = jnp.where(usable, jnp.exp(masked - updated[..., None, None]), 0.0)
        rescale = jnp.exp(running - updated)
        weight_sum = weight_sum * rescale + jnp.sum(weights, axis=(3, 4))
        rounded = weights.astype(jnp.bfloat16)
        weighted = weighted * rescale[..., None] + jnp.einsum(
            "rkhgp,gpkd->rkhd", rounded, value_block, preferred_element_type=jnp.float32
        )
        return (updated, weight_sum, weighted)

    initial = (
        jnp.full((row_count, kv_dev, repeat), FAR_BELOW, jnp.float32),
        jnp.zeros((row_count, kv_dev, repeat), jnp.float32),
        jnp.zeros((row_count, kv_dev, repeat, HD), jnp.float32),
    )
    running, weight_sum, weighted = lax.fori_loop(0, blocks, key_step, initial)
    bounded = jnp.maximum(weight_sum, 1.0)
    normalized = jnp.where(owned[:, None, None, None], weighted / bounded[..., None], 0.0).reshape(
        row_count, heads_dev * HD
    )
    log_total = jnp.where(owned[:, None, None], running + jnp.log(bounded), 0.0).reshape(
        row_count, heads_dev
    )
    return (normalized, log_total)


def body(
    query,
    new_key,
    new_value,
    prefix_key,
    prefix_value,
    suffix_key,
    suffix_value,
    group_ids,
    prompt_len,
    suffix_len,
    o_weight,
    residual,
    norm_gain,
):
    req_dev = query.shape[0]
    heads_dev = query.shape[1] // HD
    kv_dev = new_key.shape[1] // HD
    repeat = heads_dev // kv_dev
    groups_dev = prefix_key.shape[0]
    prompt_max = prefix_key.shape[1]
    suffix_max = suffix_key.shape[1]
    block_len = min(512, prompt_max)
    score_scale = 1.0 / math.sqrt(HD)
    places = lax.axis_size("req")
    device = lax.axis_index("req")
    first_group = device * groups_dev
    own_suffix = lax.dynamic_slice_in_dim(suffix_len, device * req_dev, req_dev)
    blocks = prompt_max // block_len
    capacity = max(2, req_dev // places)
    slot_total = places * capacity
    all_groups = group_ids.reshape(places, 1, req_dev)
    all_suffix = suffix_len.reshape(places, 1, req_dev)
    all_rows = (
        jnp.arange(places, dtype=jnp.int32)[:, None] * req_dev
        + jnp.arange(req_dev, dtype=jnp.int32)[None, :]
    ).reshape(places, 1, req_dev)
    is_mine = (group_ids // groups_dev).reshape(places, req_dev) == device
    slot_order = jnp.cumsum(is_mine.astype(jnp.int32), axis=1) - 1
    slot_pick = is_mine[:, None, :] & (
        slot_order[:, None, :] == jnp.arange(capacity, dtype=jnp.int32)[None, :, None]
    )
    filled = jnp.any(slot_pick, axis=2)
    slot_group = jnp.where(
        filled, jnp.sum(jnp.where(slot_pick, all_groups, 0), axis=2), -1
    ).reshape(slot_total)
    slot_suffix = jnp.sum(jnp.where(slot_pick, all_suffix, 0), axis=2).reshape(slot_total)
    slot_row = jnp.where(filled, jnp.sum(jnp.where(slot_pick, all_rows, 0), axis=2), -1).reshape(
        slot_total
    )
    own_groups = lax.dynamic_slice_in_dim(group_ids, device * req_dev, req_dev)
    own_holder = own_groups // groups_dev
    same_holder = own_holder[:, None] == own_holder[None, :]
    earlier = (
        jnp.arange(req_dev, dtype=jnp.int32)[None, :]
        < jnp.arange(req_dev, dtype=jnp.int32)[:, None]
    )
    own_rank = jnp.sum(same_holder & earlier, axis=1).astype(jnp.int32)
    own_slot = own_holder * capacity + own_rank
    send_pick = own_slot[None, :] == jnp.arange(slot_total, dtype=jnp.int32)[:, None]
    send_query = jnp.dot(
        send_pick.astype(jnp.bfloat16), query, preferred_element_type=jnp.float32
    ).astype(jnp.bfloat16)
    compact = lax.all_to_all(
        send_query.reshape(places, capacity, heads_dev * HD), "req", 0, 0, tiled=True
    ).reshape(slot_total, heads_dev * HD)
    part_out, part_log = prefix_attend(
        compact, slot_group, slot_suffix, prefix_key, prefix_value, prompt_len, first_group, blocks
    )
    packed = jnp.concatenate([part_out, part_log], axis=1)
    returned = lax.all_to_all(
        packed.reshape(places, capacity, packed.shape[1]), "req", 0, 0, tiled=True
    ).reshape(slot_total, packed.shape[1])
    picked = returned[own_slot]
    prefix_out = picked[:, : heads_dev * HD]
    prefix_log = picked[:, heads_dev * HD :]
    queries = query.reshape(req_dev, kv_dev, repeat, HD)
    key_rows = suffix_key.reshape(req_dev, suffix_max, kv_dev, HD)
    value_rows = suffix_value.reshape(req_dev, suffix_max, kv_dev, HD)
    scores = (
        jnp.einsum("rkhd,rjkd->rkhj", queries, key_rows, preferred_element_type=jnp.float32)
        * score_scale
    )
    own_score = (
        jnp.einsum(
            "rkhd,rkd->rkh",
            queries,
            new_key.reshape(req_dev, kv_dev, HD),
            preferred_element_type=jnp.float32,
        )
        * score_scale
    )
    usable = (jnp.arange(suffix_max, dtype=jnp.int32)[None, :] < own_suffix[:, None])[
        :, None, None, :
    ]
    masked = jnp.where(usable, scores, FAR_BELOW)
    running = jnp.maximum(jnp.max(masked, axis=-1), own_score)
    weights = jnp.where(usable, jnp.exp(masked - running[..., None]), 0.0)
    own_weight = jnp.exp(own_score - running)
    weight_sum = jnp.sum(weights, axis=-1) + own_weight
    weighted = jnp.einsum(
        "rkhj,rjkd->rkhd",
        weights.astype(jnp.bfloat16),
        value_rows,
        preferred_element_type=jnp.float32,
    )
    own_rounded = own_weight.astype(jnp.bfloat16).astype(jnp.float32)
    weighted = weighted + own_rounded[..., None] * new_value.reshape(req_dev, kv_dev, 1, HD).astype(
        jnp.float32
    )
    local_out = weighted / weight_sum[..., None]
    local_log = running + jnp.log(weight_sum)
    prefix_out = prefix_out.reshape(req_dev, kv_dev, repeat, HD)
    prefix_log = prefix_log.reshape(req_dev, kv_dev, repeat)
    combined = jnp.logaddexp(prefix_log, local_log)
    attended = (
        prefix_out * jnp.exp(prefix_log - combined)[..., None]
        + local_out * jnp.exp(local_log - combined)[..., None]
    )
    attended = attended.reshape(req_dev, heads_dev * HD).astype(jnp.bfloat16)
    partial_value = jnp.dot(attended, o_weight, preferred_element_type=jnp.float32)
    proj = lax.psum(partial_value, "tp")
    summed = residual.astype(jnp.float32) + proj
    hidden = summed.astype(jnp.bfloat16)
    inverse = lax.rsqrt(jnp.mean(summed * summed, axis=-1, keepdims=True) + NORM_EPS)
    normed = (summed * inverse * norm_gain.astype(jnp.float32)[None, :]).astype(jnp.bfloat16)
    return (hidden, normed)


def solution(mesh):
    placed = (
        P("req", "tp"),
        P("req", "tp"),
        P("req", "tp"),
        P("req", None, "tp"),
        P("req", None, "tp"),
        P("req", None, "tp"),
        P("req", None, "tp"),
        P(),
        P("req"),
        P(),
        P("tp", None),
        P("req", None),
        P(),
    )
    return jax.shard_map(
        body,
        mesh=mesh,
        in_specs=placed,
        out_specs=(P("req", None), P("req", None)),
        check_vma=False,
    )
```

profile of v0, /device:TPU:2, one launch (start us, length us, event | category | flops | bytes accessed | tf_op | source)
XLA Modules:
  0.0 179.4 jit_solution(5152903580054257857)
XLA Ops:
  7.2 0.8 and_select_fusion
  8.2 0.8 compare_select_fusion
  9.0 0.9 convolution_convert_fusion
  10.5 7.6 %all-to-all-start = ((bf16[32,2,512]{2,1,0:T(2,128)(2,1)}), bf16[32,2,512]{2,1,0:T(2,128)(2,1)S(1)}, u32[]{:S(2)}, u32[]{:S(2)}) async-start(bf16[32,2,512]{2,1,0:T(2,128)(2,1)} %reshape.348), calls=%async_computation | async-start | bytes 131072 | tf_op jit(solution)/shard_map/all_to_all | solution.py:140
  19.1 0.8 broadcast_in_dim.176
  19.8 0.8 broadcast_in_dim.186
  20.6 0.8 dynamic_slice.21
  21.4 0.7 reshape.351
  23.1 0.7 fusion.49
  23.8 0.8 fusion.43
  25.4 50.1 %while.18 = (s32[]{:T(128)}, f32[64,1,4]{0,2,1:T(4,128)S(1)}, f32[64,1,4]{0,2,1:T(4,128)S(1)}, f32[64,1,4,128]{3,0,2,1:T(8,128)S(1)}, s32[2]{0:T(128)}, /*index=...) while((s32[]{:T(128)}, f32[64,1,4]{0,2,1:T(4,128)S(1)}, ...), condition=%wide.region_9.10_spmd.clone, body=%wide.region_6.9_spmd.clone.sunk | while | flops 136876160 | bytes 4351959 | solution.py:66
  25.6 0.8 broadcast_compare_fusion.5
  26.5 1.4 fusion.68
  27.9 1.4 fusion.71
  29.8 0.7 broadcast_compare_fusion.5
  30.7 1.4 fusion.68
  32.1 1.4 fusion.71
  34.0 0.7 broadcast_compare_fusion.5
  34.8 1.4 fusion.68
  36.2 1.4 fusion.71
  38.2 0.7 broadcast_compare_fusion.5
  39.0 1.4 fusion.68
  40.4 1.4 fusion.71
  42.3 0.7 broadcast_compare_fusion.5
  43.2 1.4 fusion.68
  44.6 1.4 fusion.71
  46.5 0.7 broadcast_compare_fusion.5
  47.4 1.4 fusion.68
  48.7 1.4 fusion.71
  51.5 1.4 fusion.68
  52.9 1.4 fusion.71
  55.7 1.4 fusion.68
  57.1 1.4 fusion.71
  59.9 1.4 fusion.68
  61.2 1.4 fusion.71
  64.0 1.4 fusion.68
  65.4 1.4 fusion.71
  68.2 1.4 fusion.68
  69.6 1.4 fusion.71
  72.4 1.4 fusion.68
  73.7 1.4 fusion.71
  76.0 0.7 pad_maximum_fusion
  76.7 7.4 %all-to-all-start.1 = ((f32[32,2,516]{2,1,0:T(2,128)}), f32[32,2,516]{2,1,0:T(2,128)S(1)}, u32[]{:S(2)}, u32[]{:S(2)}) async-start(f32[32,2,516]{2,1,0:T(2,128)} %pad_maximum_fusion), calls=%async_computation.1 | async-start | bytes 327680 | tf_op jit(solution)/shard_map/all_to_all | solution.py:147
  84.4 6.6 %all-to-all-done.1 = f32[32,2,516]{2,1,0:T(2,128)S(1)} async-done(((f32[32,2,516]{2,1,0:T(2,128)}), f32[32,2,516]{2,1,0:T(2,128)S(1)}, u32[]{:S(2)}, u32[]{:S(2)}) %all-to-all-start.1) | async-done | bytes 132128 | tf_op jit(solution)/shard_map/all_to_all | solution.py:147
  92.2 3.6 %fusion.30 = f32[24,4096]{1,0:T(8,128)} fusion(bf16[512,4096]{1,0:T(8,128)(2,1)} %param.25, bf16[3,8,4,128]{3,2,1,0:T(4,128)(2,1)S(1)} %bitcast.84), kind=kOutput, calls=%fused_computation.52 | convolution fusion | flops 100663296 | bytes 4612096 | tf_op jit(solution)/shard_map/dot_general | solution.py:197
  95.9 73.7 %all-reduce.2.cloned.1.call-done = f32[24,4096]{1,0:T(8,128)} async-done(((f32[24,4096]{1,0:T(8,128)}), f32[24,4096]{1,0:T(8,128)}) %all-reduce.2.cloned.1.call-update) | async-done | bytes 393232 | tf_op jit(solution)/shard_map/psum | solution.py:198
  169.6 1.2 multiply_reduce_fusion
  170.7 1.8 %multiply_convert_fusion = (bf16[24,4096]{1,0:T(8,128)(2,1)}, bf16[24,4096]{1,0:T(8,128)(2,1)}) fusion(f32[4096]{0:T(1024)S(1)} %convert_element_type.66, f32[24]{0:T(128)S(1)} %add_rsqrt_fusion, f32[24,4096]{1,0:T(8,128)} %all-reduce.2.cloned.1.call-done, bf16[24,4096]{1,0:T(8,128)(2,1)S(1)} %copy-done.1), kind=kLoop, calls=%fused_computation.42 | loop fusion | flops 589824 | bytes 999520 | tf_op jit(solution)/shard_map/convert_element_type | solution.py:202
  (172 shorter events, 16.9 us)
Async XLA Ops:
  7.2 17.5 %copy-start = (bf16[24,128,128]{2,1,0:T(8,128)(2,1)S(1)}, bf16[24,128,128]{2,1,0:T(8,128)(2,1)}, u32[]{:S(2)}) copy-start(bf16[24,128,128]{2,1,0:T(8,128)(2,1)} %param.20) | copy-start | bytes 2359300
  10.5 14.8 %all-to-all-start = ((bf16[32,2,512]{2,1,0:T(2,128)(2,1)}), bf16[32,2,512]{2,1,0:T(2,128)(2,1)S(1)}, u32[]{:S(2)}, u32[]{:S(2)}) async-start(bf16[32,2,512]{2,1,0:T(2,128)(2,1)} %reshape.348), calls=%async_computation | async-start | bytes 131072 | tf_op jit(solution)/shard_map/all_to_all | solution.py:140
  25.4 58.8 %copy-start.3 = (bf16[24,128]{1,0:T(8,128)(2,1)S(1)}, bf16[24,128]{1,0:T(8,128)(2,1)}, u32[]{:S(2)}) copy-start(bf16[24,128]{1,0:T(8,128)(2,1)} %param.17) | copy-start | bytes 18436
  25.4 66.4 %copy-start.4 = (bf16[24,128,128]{2,1,0:T(8,128)(2,1)S(1)}, bf16[24,128,128]{2,1,0:T(8,128)(2,1)}, u32[]{:S(2)}) copy-start(bf16[24,128,128]{2,1,0:T(8,128)(2,1)} %param.21) | copy-start | bytes 2359300
  76.7 14.3 %all-to-all-start.1 = ((f32[32,2,516]{2,1,0:T(2,128)}), f32[32,2,516]{2,1,0:T(2,128)S(1)}, u32[]{:S(2)}, u32[]{:S(2)}) async-start(f32[32,2,516]{2,1,0:T(2,128)} %pad_maximum_fusion), calls=%async_computation.1 | async-start | bytes 327680 | tf_op jit(solution)/shard_map/all_to_all | solution.py:147
  84.1 85.5 %all-reduce.2.cloned.1.call-start = ((), (), s32[]{:S(2)}) async-start(), calls=%async_computation.2 | async-start | bytes 786432 | tf_op jit(solution)/shard_map/psum | solution.py:198
  91.8 4.0 %copy-start.2 = (bf16[4096]{0:T(1024)(128)(2,1)S(1)}, bf16[4096]{0:T(1024)(128)(2,1)}, u32[]{:S(2)}) copy-start(bf16[4096]{0:T(1024)(128)(2,1)} %param.27) | copy-start | bytes 24580
  91.8 77.7 %copy-start.1 = (bf16[24,4096]{1,0:T(8,128)(2,1)S(1)}, bf16[24,4096]{1,0:T(8,128)(2,1)}, u32[]{:S(2)}) copy-start(bf16[24,4096]{1,0:T(8,128)(2,1)} %param.26) | copy-start | bytes 589828
Sparse Core Ops, SparseCore 0:
  96.0 73.5 all-reduce.1
where the time goes:
time: 181 us; the launch traced here: 179 us
  waiting for transfers between devices  80.3 us (44%)
  matrix products  39.3 us (22%)
  other arithmetic  23.8 us (13%)
  starting transfers between devices  15 us (8%)
  between operations  14.3 us (8%)
  local copies, waits for them, and re-layouts  5.63 us (3%)
    psum x1, waiting for transfers between devices, body(): proj = lax.psum(partial_value, 'tp')  73.7 us
    dot_general x12, matrix products, key_step(): jnp.einsum('rkhgp,gpkd->rkhd', rounded, value_block, preferred_element_ty...  16.7 us
    dot_general x12, matrix products, key_step(): jnp.einsum('rkhd,gpkd->rkhgp', queries, key_block, preferred_element_type...  16.3 us
    lt x12, other arithmetic, key_step(): inside = positions[None, :] < prompt_len[:, None]  8.84 us
    all_to_all x1, starting transfers between devices, body(): lax.all_to_all(send_query.reshape(places, capacity, heads_dev * HD), 'req...  7.62 us
    all_to_all x1, starting transfers between devices, body(): lax.all_to_all(packed.reshape(places, capacity, packed.shape[1]), 'req',...  7.38 us
    all_to_all x1, waiting for transfers between devices, body(): lax.all_to_all(packed.reshape(places, capacity, packed.shape[1]), 'req',...  6.6 us
    reduce_sum x12, other arithmetic, key_step(): weight_sum = weight_sum * rescale + jnp.sum(weights, axis=(3, 4))  4.33 us
  transfers between devices with their start and end apart: 3, of which 2 were waited for; matrix products, arithmetic and copies ran while one was open for 4% of the time, Pallas kernels for 0%

commit v1 on v0

--- a/solution.py
+++ b/solution.py
@@ -195,7 +195,7 @@
     )
     attended = attended.reshape(req_dev, heads_dev * HD).astype(jnp.bfloat16)
     partial_value = jnp.dot(attended, o_weight, preferred_element_type=jnp.float32)
-    proj = lax.psum(partial_value, "tp")
+    proj = lax.all_gather(partial_value, "tp").sum(axis=0)
     summed = residual.astype(jnp.float32) + proj
     hidden = summed.astype(jnp.bfloat16)
     inverse = lax.rsqrt(jnp.mean(summed * summed, axis=-1, keepdims=True) + NORM_EPS)

time: 181 us -> 153 us (0.85)
  waiting for transfers between devices: 80.3 us -> 51.9 us
    psum x1 -> x0, waiting for transfers between devices: 73.7 us -> none  [body(): proj = lax.psum(partial_value, 'tp')]
    all_gather x0 -> x1, waiting for transfers between devices: none -> 45.3 us  [body(): proj = lax.all_gather(partial_value, 'tp').sum(axis=0)]
    reduce_sum x0 -> x1, other arithmetic: none -> 2.08 us  [body(): proj = lax.all_gather(partial_value, 'tp').sum(axis=0)]
  transfers between devices with their start and end apart: 3 -> 3, of which waited for: 2 -> 2; matrix products, arithmetic and copies ran while one was open for 4% -> 5% of each run, Pallas kernels for 0% -> 0%
where the time goes in v1:
time: 153 us; the launch traced here: 151 us
  waiting for transfers between devices  51.9 us (34%)
  matrix products  39.3 us (26%)
  other arithmetic  23.9 us (16%)
  starting transfers between devices  15 us (10%)
  between operations  14.4 us (9%)
  local copies, waits for them, and re-layouts  5.63 us (4%)
    all_gather x1, waiting for transfers between devices, body(): proj = lax.all_gather(partial_value, 'tp').sum(axis=0)  45.3 us
    dot_general x12, matrix products, key_step(): jnp.einsum('rkhgp,gpkd->rkhd', rounded, value_block, preferred_element_ty...  16.7 us
    dot_general x12, matrix products, key_step(): jnp.einsum('rkhd,gpkd->rkhgp', queries, key_block, preferred_element_type...  16.3 us
    lt x12, other arithmetic, key_step(): inside = positions[None, :] < prompt_len[:, None]  8.84 us
    all_to_all x1, starting transfers between devices, body(): lax.all_to_all(send_query.reshape(places, capacity, heads_dev * HD), 'req...  7.62 us
    all_to_all x1, starting transfers between devices, body(): lax.all_to_all(packed.reshape(places, capacity, packed.shape[1]), 'req',...  7.39 us
    all_to_all x1, waiting for transfers between devices, body(): lax.all_to_all(packed.reshape(places, capacity, packed.shape[1]), 'req',...  6.6 us
    reduce_sum x12, other arithmetic, key_step(): weight_sum = weight_sum * rescale + jnp.sum(weights, axis=(3, 4))  4.33 us
  transfers between devices with their start and end apart: 3, of which 2 were waited for; matrix products, arithmetic and copies ran while one was open for 5% of the time, Pallas kernels for 0%

profile of v1, /device:TPU:2, one launch (start us, length us, event | category | flops | bytes accessed | tf_op | source)
XLA Modules:
  0.0 151.1 jit_solution(13632689863993866610)
XLA Ops:
  7.2 0.8 and_select_fusion
  8.2 0.8 compare_select_fusion
  9.0 0.9 convolution_convert_fusion
  10.5 7.6 %all-to-all-start = ((bf16[32,2,512]{2,1,0:T(2,128)(2,1)}), bf16[32,2,512]{2,1,0:T(2,128)(2,1)S(1)}, u32[]{:S(2)}, u32[]{:S(2)}) async-start(bf16[32,2,512]{2,1,0:T(2,128)(2,1)} %reshape.348), calls=%async_computation | async-start | bytes 131072 | tf_op jit(solution)/shard_map/all_to_all | solution.py:140
  19.1 0.8 broadcast_in_dim.176
  19.8 0.8 broadcast_in_dim.186
  20.6 0.8 dynamic_slice.21
  21.4 0.7 reshape.351
  23.1 0.7 fusion.49
  23.8 0.8 fusion.43
  25.4 50.1 %while.18 = (s32[]{:T(128)}, f32[64,1,4]{0,2,1:T(4,128)S(1)}, f32[64,1,4]{0,2,1:T(4,128)S(1)}, f32[64,1,4,128]{3,0,2,1:T(8,128)S(1)}, s32[2]{0:T(128)}, /*index=...) while((s32[]{:T(128)}, f32[64,1,4]{0,2,1:T(4,128)S(1)}, ...), condition=%wide.region_9.10_spmd.clone, body=%wide.region_6.9_spmd.clone.sunk | while | flops 136876160 | bytes 4351959 | solution.py:66
  25.6 0.8 broadcast_compare_fusion.5
  26.5 1.4 fusion.68
  27.9 1.4 fusion.71
  29.8 0.7 broadcast_compare_fusion.5
  30.7 1.4 fusion.68
  32.1 1.4 fusion.71
  34.0 0.7 broadcast_compare_fusion.5
  34.8 1.4 fusion.68
  36.2 1.4 fusion.71
  38.1 0.7 broadcast_compare_fusion.5
  39.0 1.4 fusion.68
  40.4 1.4 fusion.71
  42.3 0.7 broadcast_compare_fusion.5
  43.2 1.4 fusion.68
  44.6 1.4 fusion.71
  46.5 0.7 broadcast_compare_fusion.5
  47.3 1.4 fusion.68
  48.7 1.4 fusion.71
  51.5 1.4 fusion.68
  52.9 1.4 fusion.71
  55.7 1.4 fusion.68
  57.1 1.4 fusion.71
  59.8 1.4 fusion.68
  61.2 1.4 fusion.71
  64.0 1.4 fusion.68
  65.4 1.4 fusion.71
  68.2 1.4 fusion.68
  69.5 1.4 fusion.71
  72.3 1.4 fusion.68
  73.7 1.4 fusion.71
  75.9 0.7 pad_maximum_fusion
  76.7 7.4 %all-to-all-start.1 = ((f32[32,2,516]{2,1,0:T(2,128)}), f32[32,2,516]{2,1,0:T(2,128)S(1)}, u32[]{:S(2)}, u32[]{:S(2)}) async-start(f32[32,2,516]{2,1,0:T(2,128)} %pad_maximum_fusion), calls=%async_computation.1 | async-start | bytes 327680 | tf_op jit(solution)/shard_map/all_to_all | solution.py:147
  84.3 6.6 %all-to-all-done.1 = f32[32,2,516]{2,1,0:T(2,128)S(1)} async-done(((f32[32,2,516]{2,1,0:T(2,128)}), f32[32,2,516]{2,1,0:T(2,128)S(1)}, u32[]{:S(2)}, u32[]{:S(2)}) %all-to-all-start.1) | async-done | bytes 132128 | tf_op jit(solution)/shard_map/all_to_all | solution.py:147
  92.2 3.6 %fusion.30 = f32[24,4096]{1,0:T(8,128)} fusion(bf16[512,4096]{1,0:T(8,128)(2,1)} %param.25, bf16[3,8,4,128]{3,2,1,0:T(4,128)(2,1)S(1)} %bitcast.86), kind=kOutput, calls=%fused_computation.52 | convolution fusion | flops 100663296 | bytes 4612096 | tf_op jit(solution)/shard_map/dot_general | solution.py:197
  95.9 45.3 %all-gather.3.cloned.1.call-done = f32[192,4096]{1,0:T(8,128)} async-done(((f32[24,4096]{1,0:T(8,128)}), f32[192,4096]{1,0:T(8,128)}) %all-gather.3.cloned.1.call-update) | async-done | bytes 3145744 | tf_op jit(solution)/shard_map/all_gather | solution.py:198
  141.2 2.1 %reduce_sum.81 = f32[24,4096]{1,0:T(8,128)S(1)} reduce(f32[8,24,4096]{2,1,0:T(8,128)} %bitcast.80, f32[]{:T(128)} %constant.121.clone.1), dimensions={0}, to_apply=%region_12.13 | reduce | flops 688128 | bytes 3538948 | tf_op jit(solution)/shard_map/reduce_sum | solution.py:198
  143.5 0.8 multiply_convert_fusion
  (173 shorter events, 17.0 us)
Async XLA Ops:
  7.2 17.5 %copy-start = (bf16[24,128,128]{2,1,0:T(8,128)(2,1)S(1)}, bf16[24,128,128]{2,1,0:T(8,128)(2,1)}, u32[]{:S(2)}) copy-start(bf16[24,128,128]{2,1,0:T(8,128)(2,1)} %param.20) | copy-start | bytes 2359300
  10.5 14.8 %all-to-all-start = ((bf16[32,2,512]{2,1,0:T(2,128)(2,1)}), bf16[32,2,512]{2,1,0:T(2,128)(2,1)S(1)}, u32[]{:S(2)}, u32[]{:S(2)}) async-start(bf16[32,2,512]{2,1,0:T(2,128)(2,1)} %reshape.348), calls=%async_computation | async-start | bytes 131072 | tf_op jit(solution)/shard_map/all_to_all | solution.py:140
  25.4 58.7 %copy-start.3 = (bf16[24,128]{1,0:T(8,128)(2,1)S(1)}, bf16[24,128]{1,0:T(8,128)(2,1)}, u32[]{:S(2)}) copy-start(bf16[24,128]{1,0:T(8,128)(2,1)} %param.17) | copy-start | bytes 18436
  25.4 66.4 %copy-start.4 = (bf16[24,128,128]{2,1,0:T(8,128)(2,1)S(1)}, bf16[24,128,128]{2,1,0:T(8,128)(2,1)}, u32[]{:S(2)}) copy-start(bf16[24,128,128]{2,1,0:T(8,128)(2,1)} %param.21) | copy-start | bytes 2359300
  76.7 14.3 %all-to-all-start.1 = ((f32[32,2,516]{2,1,0:T(2,128)}), f32[32,2,516]{2,1,0:T(2,128)S(1)}, u32[]{:S(2)}, u32[]{:S(2)}) async-start(f32[32,2,516]{2,1,0:T(2,128)} %pad_maximum_fusion), calls=%async_computation.1 | async-start | bytes 327680 | tf_op jit(solution)/shard_map/all_to_all | solution.py:147
  84.1 57.1 %all-gather.3.cloned.1.call-start = ((), (), s32[]{:S(2)}) async-start(), calls=%async_computation.2 | async-start | bytes 3538944 | tf_op jit(solution)/shard_map/all_gather | solution.py:198
  91.8 4.1 %copy-start.2 = (bf16[4096]{0:T(1024)(128)(2,1)S(1)}, bf16[4096]{0:T(1024)(128)(2,1)}, u32[]{:S(2)}) copy-start(bf16[4096]{0:T(1024)(128)(2,1)} %param.27) | copy-start | bytes 24580
  92.2 51.1 %copy-start.1 = (bf16[24,4096]{1,0:T(8,128)(2,1)S(1)}, bf16[24,4096]{1,0:T(8,128)(2,1)}, u32[]{:S(2)}) copy-start(bf16[24,4096]{1,0:T(8,128)(2,1)} %param.26) | copy-start | bytes 589828
Sparse Core Ops, SparseCore 0:
  96.0 45.1 all-gather.2
